TPU v7x, 32 devices: a whole 2x2x4 slice. The times are simulated.
32 devices in a mesh: ctx: 8 (over z, x), tp: 4 (over y, core).
Axes of the slice: x: 2, y: 2, z: 4, core: 2. Of those that a mesh axis runs over, the one named last changes fastest.
Arguments:
- tokens: bfloat16 [2048, 16384], P('ctx', 'tp')
- document: int32 [2048], P('ctx'), may hold values from 0 to 5, as said below
- place: int32 [2048], P('ctx'), may hold values from 0 to 1023, as said below
- w_qkv: bfloat16 [1280, 16384], P(None, 'tp')
- w_out: bfloat16 [1024, 16384], P(None, 'tp'), may hold values from -0.1875 to 0.1875
- grad_out: bfloat16 [2048, 16384], P('ctx', 'tp'), may hold values from -6 to 6
Outputs:
- out: bfloat16 [2048, 16384], P('ctx', 'tp')
- grad_x: bfloat16 [2048, 16384], P('ctx', 'tp')
- grad_w_qkv: float32 [1280, 16384], P('ctx', 'tp')
- grad_w_out: float32 [1024, 16384], P('ctx', 'tp')
Inputs may be any that keep to these rules, and one draw needn't show every extreme that they name: Each document's tokens carry the positions 0 to its length minus 1, each once; one document holds 1024 tokens. `place`: position of a token within its document, as described for document.
All inputs are finite; a program needn't handle non-finite values.
Results may differ from a plain program's by a relative error of at most 0.028.
Values may be sent and summed in bfloat16 or wider, within the bound.
No kernel may reach another device: no remote copies, remote signals or barrier semaphores. Data moves between devices by JAX's collectives and lax.ppermute only.
A program may use at most 128 MiB of HBM per device.

v0:
```python
import functools
import math
import jax
import jax.numpy as jnp
from jax import lax
from jax.sharding import PartitionSpec as P

HD = 128
HQ = 8
THETA = 500000.0
NEG = -1e30
PIECE = 64


def angles(place, width):
    half = width // 2
    freq = THETA ** (-(jnp.arange(half, dtype=jnp.float32) * 2.0 / width))
    turn = place.astype(jnp.float32)[:, None] * freq[None, :]
    return (jnp.cos(turn), jnp.sin(turn))


def rotate(vector, cosine, sine):
    half = vector.shape[-1] // 2
    first = vector[..., :half]
    second = vector[..., half:]
    return jnp.concatenate(
        [first * cosine - second * sine, second * cosine + first * sine], axis=-1
    )


def against(left, right):
    return lax.dot_general(
        left, right, (((1,), (1,)), ((), ())), preferred_element_type=jnp.float32
    )


def across(left, right):
    return lax.dot_general(
        left, right, (((0,), (0,)), ((), ())), preferred_element_type=jnp.float32
    )


def ring_of(mesh):
    count = mesh.shape["ctx"]
    try:
        grid = mesh.devices.reshape(count, -1)
        coords = [tuple(grid[i, 0].coords) for i in range(count)]
    except Exception:
        return list(range(count))
    varying = [d for d in range(len(coords[0])) if len({c[d] for c in coords}) > 1]
    if len(varying) == 1:
        return sorted(range(count), key=lambda i: coords[i][varying[0]])
    if len(varying) != 2:
        return list(range(count))
    for short, long in (varying, varying[::-1]):
        levels = sorted({c[short] for c in coords})
        if len(levels) == 2:
            there = sorted(
                (i for i in range(count) if coords[i][short] == levels[0]),
                key=lambda i: coords[i][long],
            )
            back = sorted(
                (i for i in range(count) if coords[i][short] == levels[1]),
                key=lambda i: -coords[i][long],
            )
            return there + back
    return list(range(count))


def ring_scatter(partial, ring, axis):
    count = len(ring)
    where = [0] * count
    for spot, member in enumerate(ring):
        where[member] = spot
    spot = jnp.asarray(where, jnp.int32)[lax.axis_index(axis)]
    order = jnp.asarray(ring, jnp.int32)
    rows = partial.shape[0] // count
    half = partial.shape[1] // 2
    blocks = partial.reshape(count, rows, partial.shape[1])
    left = blocks[:, :, :half]
    right = blocks[:, :, half:]

    def block(side, offset):
        return lax.dynamic_index_in_dim(side, order[(spot + offset) % count], 0, keepdims=False)

    forward = [(ring[p], ring[(p + 1) % count]) for p in range(count)]
    backward = [(ring[p], ring[(p - 1) % count]) for p in range(count)]
    send_left = block(left, count - 1)
    send_right = block(right, 1)
    for step in range(count - 1):
        got_left = lax.ppermute(send_left.astype(jnp.bfloat16), axis, forward)
        got_right = lax.ppermute(send_right.astype(jnp.bfloat16), axis, backward)
        send_left = got_left.astype(jnp.float32) + block(left, 2 * count - step - 2)
        send_right = got_right.astype(jnp.float32) + block(right, step + 2)
    return jnp.concatenate([send_left, send_right], axis=1)


def ring_spot(ring, axis):
    where = [0] * len(ring)
    for spot, member in enumerate(ring):
        where[member] = spot
    return jnp.asarray(where, jnp.int32)[lax.axis_index(axis)]


def ring_gather(value, ring, axis):
    count = len(ring)
    forward = [(ring[p], ring[(p + 1) % count]) for p in range(count)]
    backward = [(ring[p], ring[(p - 1) % count]) for p in range(count)]
    ahead = count // 2
    behind = count - 1 - ahead
    got = [value] + [None] * (count - 1)
    from_left = value
    from_right = value
    for step in range(max(ahead, behind)):
        if step < ahead:
            from_left = lax.ppermute(from_left, axis, forward)
            got[count - step - 1] = from_left
        if step < behind:
            from_right = lax.ppermute(from_right, axis, backward)
            got[step + 1] = from_right
    return jnp.stack(got, axis=0)


def ring_scatter_relative(partial, ring, axis):
    count = len(ring)
    rows = partial.shape[0] // count
    half = partial.shape[1] // 2
    blocks = partial.reshape(count, rows, partial.shape[1])
    left = blocks[:, :, :half]
    right = blocks[:, :, half:]
    forward = [(ring[p], ring[(p + 1) % count]) for p in range(count)]
    backward = [(ring[p], ring[(p - 1) % count]) for p in range(count)]
    send_left = left[count - 1]
    send_right = right[1 % count]
    for step in range(count - 1):
        got_left = lax.ppermute(send_left.astype(jnp.bfloat16), axis, forward)
        got_right = lax.ppermute(send_right.astype(jnp.bfloat16), axis, backward)
        send_left = got_left.astype(jnp.float32) + left[(2 * count - step - 2) % count]
        send_right = got_right.astype(jnp.float32) + right[(step + 2) % count]
    return jnp.concatenate([send_left, send_right], axis=1)


class Ring:

    def __init__(self, partial, ring, axis):
        count = len(ring)
        self.count = count
        self.axis = axis
        self.spot = ring_spot(ring, axis)
        self.order = jnp.asarray(ring, jnp.int32)
        rows = partial.shape[0] // count
        half = partial.shape[1] // 2
        blocks = partial.reshape(count, rows, partial.shape[1])
        self.left = blocks[:, :, :half]
        self.right = blocks[:, :, half:]
        self.forward = [(ring[p], ring[(p + 1) % count]) for p in range(count)]
        self.backward = [(ring[p], ring[(p - 1) % count]) for p in range(count)]
        self.state = (self.block(self.left, count - 1), self.block(self.right, 1))
        self.done = 0

    def block(self, side, offset):
        index = self.order[(self.spot + offset) % self.count]
        return lax.dynamic_index_in_dim(side, index, 0, keepdims=False)

    def advance(self, upto):
        count = self.count
        send_left, send_right = self.state
        for step in range(self.done, min(upto, count - 1)):
            got_left = lax.ppermute(send_left.astype(jnp.bfloat16), self.axis, self.forward)
            got_right = lax.ppermute(send_right.astype(jnp.bfloat16), self.axis, self.backward)
            send_left = got_left.astype(jnp.float32) + self.block(self.left, 2 * count - step - 2)
            send_right = got_right.astype(jnp.float32) + self.block(self.right, step + 2)
            self.done = step + 1
        self.state = (send_left, send_right)
        return self

    def result(self):
        self.advance(self.count - 1)
        return jnp.concatenate(list(self.state), axis=1)


def tp_project(partial, rows_mine, split, axis):
    rank = lax.axis_index(axis)
    core = rank % 2
    near = [(i, i ^ 1) for i in range(4)]
    far = [(i, i ^ 2) for i in range(4)]
    chip = partial + lax.ppermute(partial, axis, near)
    head = chip[:, :split]
    tail = chip[:, split:]
    half_rows = tail.shape[0] // 2
    mine = lax.dynamic_slice_in_dim(head, rank * rows_mine, rows_mine, 0)
    theirs = lax.dynamic_slice_in_dim(head, (rank ^ 2) * rows_mine, rows_mine, 0)
    own_head = mine + lax.ppermute(theirs, axis, far)
    tail_half = lax.dynamic_slice_in_dim(tail, core * half_rows, half_rows, 0)
    tail_half = tail_half + lax.ppermute(tail_half, axis, far)
    other_half = lax.ppermute(tail_half, axis, near)
    first = jnp.where(core == 0, tail_half, other_half)
    second = jnp.where(core == 0, other_half, tail_half)
    return (own_head, jnp.concatenate([first, second], axis=0))


def tp_scatter(partial, rows_mine, axis):
    rank = lax.axis_index(axis)
    far = [(i, i ^ 2) for i in range(4)]
    near = [(i, i ^ 1) for i in range(4)]
    pair_rows = 2 * rows_mine
    chip = rank // 2
    kept = lax.dynamic_slice_in_dim(partial, chip * pair_rows, pair_rows, 0)
    sent = lax.dynamic_slice_in_dim(partial, (1 - chip) * pair_rows, pair_rows, 0)
    kept = kept.astype(jnp.float32) + lax.ppermute(sent.astype(jnp.bfloat16), axis, far).astype(
        jnp.float32
    )
    core = rank % 2
    mine = lax.dynamic_slice_in_dim(kept, core * rows_mine, rows_mine, 0)
    other = lax.dynamic_slice_in_dim(kept, (1 - core) * rows_mine, rows_mine, 0)
    return mine + lax.ppermute(other.astype(jnp.bfloat16), axis, near).astype(jnp.float32)


def direct_gather(value, axis):
    count = lax.axis_size(axis)
    got = [value] + [None] * (count - 1)
    for shift in range(1, count):
        pairs = [(i, (i + shift) % count) for i in range(count)]
        got[count - shift] = lax.ppermute(value, axis, pairs)
    return jnp.stack(got, axis=0)


def direct_scatter(partial, axis):
    count = lax.axis_size(axis)
    rows = partial.shape[0] // count
    blocks = partial.reshape(count, rows, partial.shape[1])
    total = blocks[0]
    for shift in range(1, count):
        pairs = [(i, (i + shift) % count) for i in range(count)]
        total = total + lax.ppermute(blocks[shift].astype(jnp.bfloat16), axis, pairs).astype(
            jnp.float32
        )
    return total


def butterfly_sum(value, axis):
    count = lax.axis_size(axis)
    stride = 1
    while stride < count:
        pairs = [(i, i ^ stride) for i in range(count)]
        value = value + lax.ppermute(value, axis, pairs)
        stride *= 2
    return value


def shards(ring, tokens, document, place, w_qkv, w_out, grad_out):
    rows_ctx, slice_width = tokens.shape
    ctx_size = lax.axis_size("ctx")
    tp_size = lax.axis_size("tp")
    rows_mine = rows_ctx // tp_size
    tp_rank = lax.axis_index("tp")
    head_dim = HD
    heads = HQ
    heads_width = heads * head_dim
    pair_width = 2 * head_dim
    factor = 1.0 / math.sqrt(head_dim)
    first_row = tp_rank * rows_mine
    stacked = heads * rows_mine
    total_rows = ctx_size * rows_ctx
    grad_part = against(grad_out, w_out).astype(jnp.bfloat16)
    cosine_all, sine_all = angles(place, head_dim)
    cosine_mine = lax.dynamic_slice_in_dim(cosine_all, first_row, rows_mine, 0)
    sine_mine = lax.dynamic_slice_in_dim(sine_all, first_row, rows_mine, 0)
    query_doc = lax.dynamic_slice_in_dim(document, first_row, rows_mine, 0)
    query_place = lax.dynamic_slice_in_dim(place, first_row, rows_mine, 0)
    projected = against(tokens, w_qkv)
    if tp_size == 4 and rows_ctx % (2 * tp_size) == 0:
        query_block, pair_rows = tp_project(projected, rows_mine, heads_width, "tp")
    else:
        qkv = lax.psum(projected, "tp")
        query_block = lax.dynamic_slice_in_dim(qkv[:, :heads_width], first_row, rows_mine, 0)
        pair_rows = qkv[:, heads_width:]
    keys = rotate(pair_rows[:, :head_dim], cosine_all, sine_all).astype(jnp.bfloat16)
    values = pair_rows[:, head_dim:].astype(jnp.bfloat16)
    info = jnp.concatenate([document, place // PIECE, place % PIECE], axis=0).astype(jnp.float32)
    info_rows = -(-info.shape[0] // pair_width)
    info = jnp.pad(info, (0, info_rows * pair_width - info.shape[0]))
    info = info.reshape(info_rows, pair_width).astype(jnp.bfloat16)
    packed = jnp.concatenate([keys, values], axis=1)
    packed = jnp.concatenate([packed, info], axis=0)
    gathered = direct_gather(packed, "ctx")
    if tp_size == 4 and rows_ctx % (2 * tp_size) == 0:
        grad_rows = tp_scatter(grad_part, rows_mine, "tp").astype(jnp.bfloat16)
    else:
        grad_rows = lax.psum_scatter(grad_part, "tp", scatter_dimension=0, tiled=True)
    keys_all = gathered[:, :rows_ctx, :head_dim].reshape(total_rows, head_dim)
    values_all = gathered[:, :rows_ctx, head_dim:].reshape(total_rows, head_dim)
    info_all = (
        gathered[:, rows_ctx:, :].reshape(ctx_size, info_rows * pair_width).astype(jnp.float32)
    )
    key_doc = info_all[:, :rows_ctx].reshape(total_rows)
    key_place = (
        info_all[:, rows_ctx : 2 * rows_ctx] * PIECE + info_all[:, 2 * rows_ctx : 3 * rows_ctx]
    ).reshape(total_rows)
    allowed = (query_doc.astype(jnp.float32)[:, None] == key_doc[None, :]) & (
        key_place[None, :] <= query_place.astype(jnp.float32)[:, None]
    )
    allowed = jnp.broadcast_to(allowed[None], (heads, rows_mine, total_rows)).reshape(
        stacked, total_rows
    )
    raw_query = query_block.reshape(rows_mine, heads, head_dim)
    rotated = rotate(raw_query, cosine_mine[:, None, :], sine_mine[:, None, :]).astype(jnp.bfloat16)
    queries = jnp.transpose(rotated, (1, 0, 2)).reshape(stacked, head_dim)
    scores = against(queries, keys_all) * factor
    masked = jnp.where(allowed, scores, NEG)
    top = jnp.max(masked, axis=1)
    weights = jnp.where(allowed, jnp.exp(masked - top[:, None]), 0.0)
    total = jnp.sum(weights, axis=1)
    summed = jnp.dot(weights.astype(jnp.bfloat16), values_all, preferred_element_type=jnp.float32)
    attended = (summed / total[:, None]).astype(jnp.bfloat16)
    logsum = top + jnp.log(total)
    rows_attended = jnp.transpose(attended.reshape(heads, rows_mine, head_dim), (1, 0, 2)).reshape(
        rows_mine, heads_width
    )
    piece = lax.all_gather(rows_attended, "tp", axis=0, tiled=True)
    out = jnp.dot(piece, w_out, preferred_element_type=jnp.float32).astype(jnp.bfloat16)
    out_weight_grad = across(piece, grad_out)
    grad_stack = jnp.transpose(grad_rows.reshape(rows_mine, heads, head_dim), (1, 0, 2)).reshape(
        stacked, head_dim
    )
    delta = jnp.sum(grad_stack.astype(jnp.float32) * attended.astype(jnp.float32), axis=1)
    prob = jnp.where(allowed, jnp.exp(scores - logsum[:, None]), 0.0)
    dprob = against(grad_stack, values_all)
    dscore = (prob * (dprob - delta[:, None])).astype(jnp.bfloat16)
    query_sum = jnp.dot(dscore, keys_all, preferred_element_type=jnp.float32)
    key_part = across(dscore, queries) * factor
    value_part = across(prob.astype(jnp.bfloat16), grad_stack)
    pair_all = jnp.concatenate([key_part, value_part], axis=1)
    out_ring = Ring(out_weight_grad, ring, "ctx").advance(len(ring) // 4)
    pair_grad = butterfly_sum(direct_scatter(pair_all, "ctx"), "tp")
    out_ring.state, pair_grad = lax.optimization_barrier((out_ring.state, pair_grad))
    key_raw = rotate(pair_grad[:, :head_dim], cosine_all, -sine_all)
    query_grad = jnp.transpose((query_sum * factor).reshape(heads, rows_mine, head_dim), (1, 0, 2))
    query_raw = rotate(query_grad, cosine_mine[:, None, :], -sine_mine[:, None, :]).reshape(
        rows_mine, heads_width
    )
    query_rows = lax.all_gather(query_raw.astype(jnp.bfloat16), "tp", axis=0, tiled=True)
    d_qkv = jnp.concatenate(
        [query_rows, key_raw.astype(jnp.bfloat16), pair_grad[:, head_dim:].astype(jnp.bfloat16)],
        axis=1,
    )
    grad_x = jnp.dot(d_qkv, w_qkv, preferred_element_type=jnp.float32).astype(jnp.bfloat16)
    joint_weight = across(d_qkv, tokens)
    out_ring.advance(len(ring) - 1)
    out_ring.state, joint_weight = lax.optimization_barrier((out_ring.state, joint_weight))
    grad_w_qkv = ring_scatter(joint_weight, ring, "ctx")
    grad_w_out = out_ring.result()
    return (out, grad_x, grad_w_qkv, grad_w_out)


def solution(mesh):
    return jax.shard_map(
        functools.partial(shards, ring_of(mesh)),
        mesh=mesh,
        in_specs=(P("ctx", "tp"), P("ctx"), P("ctx"), P(None, "tp"), P(None, "tp"), P("ctx", "tp")),
        out_specs=(P("ctx", "tp"), P("ctx", "tp"), P("ctx", "tp"), P("ctx", "tp")),
        check_vma=False,
    )
```

profile of v0, /device:TPU:0, one launch (start us, length us, event | category | flops | bytes accessed | tf_op | source)
XLA Modules:
  0.0 346.1 jit_solution(10542800763910754592)
XLA Ops:
  2.2 6.9 %fusion.70 = f32[256,1280]{1,0:T(8,128)S(1)} fusion(bf16[256,4096]{1,0:T(8,128)(2,1)S(1)} %copy-done, bf16[1280,4096]{1,0:T(8,128)(2,1)} %param.13), kind=kOutput, calls=%fused_computation.172 | convolution fusion | flops 2684354560 | bytes 13893632 | tf_op jit(solution)/shard_map/dot_general | solution.py:32
  9.6 6.4 %convolution_convert_fusion.2 = bf16[256,1024]{1,0:T(8,128)(2,1)S(1)} fusion(bf16[256,4096]{1,0:T(8,128)(2,1)} %param.15, bf16[1024,4096]{1,0:T(8,128)(2,1)} %param.14), kind=kOutput, calls=%fused_computation.45 | convolution fusion | flops 2147745792 | bytes 11010048 | tf_op jit(solution)/shard_map/dot_general | solution.py:32
  37.9 4.2 %collective-permute-done.1 = f32[128,256]{1,0:T(8,128)S(1)} collective-permute-done((f32[128,256]{1,0:T(8,128)S(1)}, f32[128,256]{1,0:T(8,128)S(1)}, u32[]{:S(2)}, u32[]{:S(2)}) %collective-permute-start.1) | collective-permute-done | bytes 131104 | tf_op jit(solution)/shard_map/ppermute | solution.py:195
  44.3 4.6 %collective-permute-start.3 = (bf16[259,256]{1,0:T(8,128)(2,1)S(1)}, bf16[259,256]{1,0:T(8,128)(2,1)S(1)}, u32[]{:S(2)}, u32[]{:S(2)}) collective-permute-start(bf16[259,256]{1,0:T(8,128)(2,1)S(1)} %get-tuple-element.19), channel_id=1, source_target_pairs={{0,28},{4,0},{8,4},{12,8},{16,12},{20,16},{24,20},{28,24},{1,29},{... | collective-permute-start | bytes 397832 | tf_op jit(solution)/shard_map/ppermute | solution.py:224
  49.4 3.0 collective-permute-start.6
  58.8 13.5 %collective-permute-done.6 = bf16[259,256]{1,0:T(8,128)(2,1)S(1)} collective-permute-done((bf16[259,256]{1,0:T(8,128)(2,1)S(1)}, bf16[259,256]{1,0:T(8,128)(2,1)S(1)}, u32[]{:S(2)}, u32[]{:S(2)}) %collective-permute-start.6) | collective-permute-done | bytes 132640 | tf_op jit(solution)/shard_map/ppermute | solution.py:224
  89.0 6.7 %all_gather.6 = bf16[256,1024]{1,0:T(8,128)(2,1)S(1)} all-gather(bf16[64,1024]{1,0:T(8,128)(2,1)S(1)} %bitcast.244), channel_id=1, replica_groups=mesh['ctx'=8,'tp'=4] {'tp'}, dimensions={0}, use_global_device_ids=true | all-gather | bytes 655360 | tf_op jit(solution)/shard_map/all_gather | solution.py:320
  98.2 6.3 %fusion.65 = (f32[8,128,2048]{2,1,0:T(8,128)}, f32[8,128,2048]{2,1,0:T(8,128)}) fusion(f32[8,128,4096]{2,1,0:T(8,128)S(1)} %bitcast.233), kind=kLoop, calls=%fused_computation.167 | loop fusion | bytes 33554432 | tf_op jit(solution)/shard_map/slice | solution.py:155
  106.9 2.9 collective-permute-start.23
  160.0 10.3 %collective-permute-done.31 = bf16[128,2048]{1,0:T(8,128)(2,1)S(1)} collective-permute-done((bf16[128,2048]{1,0:T(8,128)(2,1)S(1)}, bf16[128,2048]{1,0:T(8,128)(2,1)S(1)}, u32[]{:S(2)}, u32[]{:S(2)}) %collective-permute-start.31) | collective-permute-done | bytes 524320 | tf_op jit(solution)/shard_map/ppermute | solution.py:170
  175.2 9.0 %collective-permute-done.32 = bf16[128,2048]{1,0:T(8,128)(2,1)S(1)} collective-permute-done((bf16[128,2048]{1,0:T(8,128)(2,1)S(1)}, bf16[128,2048]{1,0:T(8,128)(2,1)S(1)}, u32[]{:S(2)}, u32[]{:S(2)}) %collective-permute-start.32) | collective-permute-done | bytes 524320 | tf_op jit(solution)/shard_map/ppermute | solution.py:170
  189.5 7.1 %all_gather.7 = bf16[256,1024]{1,0:T(8,128)(2,1)} all-gather(bf16[64,1024]{1,0:T(8,128)(2,1)S(1)} %copy_bitcast_fusion.1), channel_id=1, replica_groups=mesh['ctx'=8,'tp'=4] {'tp'}, dimensions={0}, use_global_device_ids=true | all-gather | bytes 655360 | tf_op jit(solution)/shard_map/all_gather | solution.py:342
  206.4 7.1 %collective-permute-done.34 = bf16[128,2048]{1,0:T(8,128)(2,1)} collective-permute-done((bf16[128,2048]{1,0:T(8,128)(2,1)}, bf16[128,2048]{1,0:T(8,128)(2,1)}, u32[]{:S(2)}, u32[]{:S(2)}) %collective-permute-start.34) | collective-permute-done | bytes 524320 | tf_op jit(solution)/shard_map/ppermute | solution.py:170
  218.9 2.9 fusion.73
  221.8 5.0 %collective-permute-done.35 = bf16[128,2048]{1,0:T(8,128)(2,1)S(1)} collective-permute-done((bf16[128,2048]{1,0:T(8,128)(2,1)S(1)}, bf16[128,2048]{1,0:T(8,128)(2,1)S(1)}, u32[]{:S(2)}, u32[]{:S(2)}) %collective-permute-start.35) | collective-permute-done | bytes 524320 | tf_op jit(solution)/shard_map/ppermute | solution.py:170
  230.9 8.1 %fusion.64 = (f32[8,160,2048]{2,1,0:T(8,128)}, f32[8,160,2048]{2,1,0:T(8,128)}) fusion(f32[8,160,4096]{2,1,0:T(8,128)S(1)} %bitcast.232), kind=kLoop, calls=%fused_computation.166 | loop fusion | bytes 41943040 | tf_op jit(solution)/shard_map/slice | solution.py:80
  244.4 9.9 %collective-permute-done.36 = bf16[160,2048]{1,0:T(8,128)(2,1)S(1)} collective-permute-done((bf16[160,2048]{1,0:T(8,128)(2,1)S(1)}, bf16[160,2048]{1,0:T(8,128)(2,1)S(1)}, u32[]{:S(2)}, u32[]{:S(2)}) %collective-permute-start.36) | collective-permute-done | bytes 655392 | tf_op jit(solution)/shard_map/ppermute | solution.py:91
  259.4 9.8 %collective-permute-done.37 = bf16[160,2048]{1,0:T(8,128)(2,1)S(1)} collective-permute-done((bf16[160,2048]{1,0:T(8,128)(2,1)S(1)}, bf16[160,2048]{1,0:T(8,128)(2,1)S(1)}, u32[]{:S(2)}, u32[]{:S(2)}) %collective-permute-start.37) | collective-permute-done | bytes 655392 | tf_op jit(solution)/shard_map/ppermute | solution.py:91
  274.1 10.0 %collective-permute-done.38 = bf16[160,2048]{1,0:T(8,128)(2,1)S(1)} collective-permute-done((bf16[160,2048]{1,0:T(8,128)(2,1)S(1)}, bf16[160,2048]{1,0:T(8,128)(2,1)S(1)}, u32[]{:S(2)}, u32[]{:S(2)}) %collective-permute-start.38) | collective-permute-done | bytes 655392 | tf_op jit(solution)/shard_map/ppermute | solution.py:91
  289.0 10.0 %collective-permute-done.39 = bf16[160,2048]{1,0:T(8,128)(2,1)S(1)} collective-permute-done((bf16[160,2048]{1,0:T(8,128)(2,1)S(1)}, bf16[160,2048]{1,0:T(8,128)(2,1)S(1)}, u32[]{:S(2)}, u32[]{:S(2)}) %collective-permute-start.39) | collective-permute-done | bytes 655392 | tf_op jit(solution)/shard_map/ppermute | solution.py:91
  303.9 7.8 %convolution_convert_fusion = bf16[256,4096]{1,0:T(8,128)(2,1)} fusion(bf16[256,1024]{1,0:T(8,128)(2,1)S(1)} %all_gather.6, bf16[1024,4096]{1,0:T(8,128)(2,1)} %param.14), kind=kOutput, calls=%fused_computation.3 | convolution fusion | flops 2148532224 | bytes 11010048 | tf_op jit(solution)/shard_map/dot_general | solution.py:321
  318.5 4.1 %convolution_convert_fusion.1 = bf16[256,4096]{1,0:T(8,128)(2,1)} fusion(bf16[256,1280]{1,0:T(8,128)(2,1)S(1)} %concatenate.45, bf16[1280,4096]{1,0:T(8,128)(2,1)S(1)} %bitcast.251), kind=kOutput, calls=%fused_computation.4 | convolution fusion | flops 2685403136 | bytes 13238272 | tf_op jit(solution)/shard_map/dot_general | solution.py:347
  322.7 7.4 %collective-permute-done.41 = bf16[160,2048]{1,0:T(8,128)(2,1)S(1)} collective-permute-done((bf16[160,2048]{1,0:T(8,128)(2,1)S(1)}, bf16[160,2048]{1,0:T(8,128)(2,1)S(1)}, u32[]{:S(2)}, u32[]{:S(2)}) %collective-permute-start.41) | collective-permute-done | bytes 655392 | tf_op jit(solution)/shard_map/ppermute | solution.py:91
  335.6 6.8 %collective-permute-done.42 = bf16[160,2048]{1,0:T(8,128)(2,1)S(1)} collective-permute-done((bf16[160,2048]{1,0:T(8,128)(2,1)S(1)}, bf16[160,2048]{1,0:T(8,128)(2,1)S(1)}, u32[]{:S(2)}, u32[]{:S(2)}) %collective-permute-start.42) | collective-permute-done | bytes 655392 | tf_op jit(solution)/shard_map/ppermute | solution.py:91
  (221 shorter events, 139.1 us)
Async XLA Ops:
  9.1 25.8 %collective-permute-start = (f32[256,1280]{1,0:T(8,128)S(1)}, f32[256,1280]{1,0:T(8,128)}, u32[]{:S(2)}, u32[]{:S(2)}) collective-permute-start(f32[256,1280]{1,0:T(8,128)S(1)} %fusion.70), channel_id=1, source_target_pairs={{0,1},{1,0},{2,3},{3,2},{4,5},{5,4},{6,7},{7,6},{8,9},{9,8},{10,11... | collective-permute-start | bytes 3932168 | tf_op jit(solution)/shard_map/ppermute | solution.py:187
  17.6 19.0 %collective-permute-start.11 = (bf16[128,1024]{1,0:T(8,128)(2,1)}, bf16[128,1024]{1,0:T(8,128)(2,1)}, u32[]{:S(2)}, u32[]{:S(2)}) collective-permute-start(bf16[128,1024]{1,0:T(8,128)(2,1)} %constant_dynamic-slice_fusion), channel_id=1, source_target_pairs={{0,2},{1,3},{2,0},{3,1},{4,6},{5,7},{6,4},{7,5},{8,10},{9,11},{10,... | collective-permute-start | bytes 786440 | tf_op jit(solution)/shard_map/ppermute | solution.py:210
  49.4 22.9 %collective-permute-start.6 = (bf16[259,256]{1,0:T(8,128)(2,1)S(1)}, bf16[259,256]{1,0:T(8,128)(2,1)S(1)}, u32[]{:S(2)}, u32[]{:S(2)}) collective-permute-start(bf16[259,256]{1,0:T(8,128)(2,1)S(1)} %get-tuple-element.19), channel_id=1, source_target_pairs={{0,16},{4,20},{8,24},{12,28},{16,0},{20,4},{24,8},{28,12},{1,17},{... | collective-permute-start | bytes 397832 | tf_op jit(solution)/shard_map/ppermute | solution.py:224
  53.0 20.7 %collective-permute-start.7 = (bf16[259,256]{1,0:T(8,128)(2,1)S(1)}, bf16[259,256]{1,0:T(8,128)(2,1)S(1)}, u32[]{:S(2)}, u32[]{:S(2)}) collective-permute-start(bf16[259,256]{1,0:T(8,128)(2,1)S(1)} %get-tuple-element.19), channel_id=1, source_target_pairs={{0,12},{4,16},{8,20},{12,24},{16,28},{20,0},{24,4},{28,8},{1,13},{... | collective-permute-start | bytes 397832 | tf_op jit(solution)/shard_map/ppermute | solution.py:224
  54.2 19.6 %collective-permute-start.8 = (bf16[259,256]{1,0:T(8,128)(2,1)S(1)}, bf16[259,256]{1,0:T(8,128)(2,1)S(1)}, u32[]{:S(2)}, u32[]{:S(2)}) collective-permute-start(bf16[259,256]{1,0:T(8,128)(2,1)S(1)} %get-tuple-element.19), channel_id=1, source_target_pairs={{0,8},{4,12},{8,16},{12,20},{16,24},{20,28},{24,0},{28,4},{1,9},{5... | collective-permute-start | bytes 397832 | tf_op jit(solution)/shard_map/ppermute | solution.py:224
  55.8 17.9 %collective-permute-start.9 = (bf16[259,256]{1,0:T(8,128)(2,1)S(1)}, bf16[259,256]{1,0:T(8,128)(2,1)S(1)}, u32[]{:S(2)}, u32[]{:S(2)}) collective-permute-start(bf16[259,256]{1,0:T(8,128)(2,1)S(1)} %get-tuple-element.19), channel_id=1, source_target_pairs={{0,4},{4,8},{8,12},{12,16},{16,20},{20,24},{24,28},{28,0},{1,5},{5... | collective-permute-start | bytes 397832 | tf_op jit(solution)/shard_map/ppermute | solution.py:224
  82.3 22.2 %collective-permute-start.17 = (bf16[256,256]{1,0:T(8,128)(2,1)}, bf16[256,256]{1,0:T(8,128)(2,1)}, u32[]{:S(2)}, u32[]{:S(2)}) collective-permute-start(bf16[256,256]{1,0:T(8,128)(2,1)} %get-tuple-element.30), channel_id=1, source_target_pairs={{0,4},{4,8},{8,12},{12,16},{16,20},{20,24},{24,28},{28,0},{1,5},{5... | collective-permute-start | bytes 393224 | tf_op jit(solution)/shard_map/ppermute | solution.py:235
  82.3 24.6 %collective-permute-start.18 = (bf16[256,256]{1,0:T(8,128)(2,1)}, bf16[256,256]{1,0:T(8,128)(2,1)}, u32[]{:S(2)}, u32[]{:S(2)}) collective-permute-start(bf16[256,256]{1,0:T(8,128)(2,1)} %get-tuple-element.36), channel_id=1, source_target_pairs={{0,8},{4,12},{8,16},{12,20},{16,24},{20,28},{24,0},{28,4},{1,9},{5... | collective-permute-start | bytes 393224 | tf_op jit(solution)/shard_map/ppermute | solution.py:235
  83.2 28.7 %collective-permute-start.19 = (bf16[256,256]{1,0:T(8,128)(2,1)}, bf16[256,256]{1,0:T(8,128)(2,1)}, u32[]{:S(2)}, u32[]{:S(2)}) collective-permute-start(bf16[256,256]{1,0:T(8,128)(2,1)} %get-tuple-element.35), channel_id=1, source_target_pairs={{0,12},{4,16},{8,20},{12,24},{16,28},{20,0},{24,4},{28,8},{1,13},{... | collective-permute-start | bytes 393224 | tf_op jit(solution)/shard_map/ppermute | solution.py:235
  86.0 25.9 %collective-permute-start.20 = (bf16[256,256]{1,0:T(8,128)(2,1)}, bf16[256,256]{1,0:T(8,128)(2,1)}, u32[]{:S(2)}, u32[]{:S(2)}) collective-permute-start(bf16[256,256]{1,0:T(8,128)(2,1)} %get-tuple-element.34), channel_id=1, source_target_pairs={{0,16},{4,20},{8,24},{12,28},{16,0},{20,4},{24,8},{28,12},{1,17},{... | collective-permute-start | bytes 393224 | tf_op jit(solution)/shard_map/ppermute | solution.py:235
  87.6 24.3 %collective-permute-start.21 = (bf16[256,256]{1,0:T(8,128)(2,1)}, bf16[256,256]{1,0:T(8,128)(2,1)}, u32[]{:S(2)}, u32[]{:S(2)}) collective-permute-start(bf16[256,256]{1,0:T(8,128)(2,1)} %get-tuple-element.33), channel_id=1, source_target_pairs={{0,20},{4,24},{8,28},{12,0},{16,4},{20,8},{24,12},{28,16},{1,21},{... | collective-permute-start | bytes 393224 | tf_op jit(solution)/shard_map/ppermute | solution.py:235
  111.9 13.9 %collective-permute-start.15 = (bf16[128,2048]{1,0:T(8,128)(2,1)}, bf16[128,2048]{1,0:T(8,128)(2,1)}, u32[]{:S(2)}, u32[]{:S(2)}) collective-permute-start(bf16[128,2048]{1,0:T(8,128)(2,1)} %fusion.31), channel_id=1, source_target_pairs={{0,4},{8,0},{16,8},{24,16},{28,24},{20,28},{12,20},{4,12},{1,5},{9... | collective-permute-start | bytes 1572872 | tf_op jit(solution)/shard_map/ppermute | solution.py:170
  116.4 14.6 %collective-permute-start.13 = (bf16[128,2048]{1,0:T(8,128)(2,1)}, bf16[128,2048]{1,0:T(8,128)(2,1)}, u32[]{:S(2)}, u32[]{:S(2)}) collective-permute-start(bf16[128,2048]{1,0:T(8,128)(2,1)} %fusion.30), channel_id=1, source_target_pairs={{0,8},{8,16},{16,24},{24,28},{28,20},{20,12},{12,4},{4,0},{1,9},{9... | collective-permute-start | bytes 1572872 | tf_op jit(solution)/shard_map/ppermute | solution.py:169
  122.3 30.6 %collective-permute-start.25 = (f32[256,256]{1,0:T(8,128)S(1)}, f32[256,256]{1,0:T(8,128)}, u32[]{:S(2)}, u32[]{:S(2)}) collective-permute-start(f32[256,256]{1,0:T(8,128)S(1)} %add.689), channel_id=1, source_target_pairs={{0,2},{1,3},{2,0},{3,1},{4,6},{5,7},{6,4},{7,5},{8,10},{9,11},{10,... | collective-permute-start | bytes 786440 | tf_op jit(solution)/shard_map/ppermute | solution.py:246
  128.1 25.8 %collective-permute-start.16 = (bf16[128,2048]{1,0:T(8,128)(2,1)}, bf16[128,2048]{1,0:T(8,128)(2,1)}, u32[]{:S(2)}, u32[]{:S(2)}) collective-permute-start(bf16[128,2048]{1,0:T(8,128)(2,1)} %fusion.26), channel_id=1, source_target_pairs={{0,4},{8,0},{16,8},{24,16},{28,24},{20,28},{12,20},{4,12},{1,5},{9... | collective-permute-start | bytes 1572872 | tf_op jit(solution)/shard_map/ppermute | solution.py:170
  133.3 22.2 %collective-permute-start.14 = (bf16[128,2048]{1,0:T(8,128)(2,1)}, bf16[128,2048]{1,0:T(8,128)(2,1)}, u32[]{:S(2)}, u32[]{:S(2)}) collective-permute-start(bf16[128,2048]{1,0:T(8,128)(2,1)} %fusion.27), channel_id=1, source_target_pairs={{0,8},{8,16},{16,24},{24,28},{28,20},{20,12},{12,4},{4,0},{1,9},{9... | collective-permute-start | bytes 1572872 | tf_op jit(solution)/shard_map/ppermute | solution.py:169
  158.8 14.4 %collective-permute-start.26 = (bf16[128,2048]{1,0:T(8,128)(2,1)S(1)}, bf16[128,2048]{1,0:T(8,128)(2,1)S(1)}, u32[]{:S(2)}, u32[]{:S(2)}) collective-permute-start(bf16[128,2048]{1,0:T(8,128)(2,1)S(1)} %bitcast_add_fusion.26), channel_id=1, source_target_pairs={{0,8},{8,16},{16,24},{24,28},{28,20},{20,12},{12,4},{4,0},{1,9},{9... | collective-permute-start | bytes 1572872 | tf_op jit(solution)/shard_map/ppermute | solution.py:169
  240.5 13.8 %collective-permute-start.36 = (bf16[160,2048]{1,0:T(8,128)(2,1)S(1)}, bf16[160,2048]{1,0:T(8,128)(2,1)S(1)}, u32[]{:S(2)}, u32[]{:S(2)}) collective-permute-start(bf16[160,2048]{1,0:T(8,128)(2,1)S(1)} %fusion.28), channel_id=1, source_target_pairs={{0,8},{8,16},{16,24},{24,28},{28,20},{20,12},{12,4},{4,0},{1,9},{9... | collective-permute-start | bytes 1966088 | tf_op jit(solution)/shard_map/ppermute | solution.py:91
  258.5 13.8 %collective-permute-start.44 = (bf16[160,2048]{1,0:T(8,128)(2,1)S(1)}, bf16[160,2048]{1,0:T(8,128)(2,1)S(1)}, u32[]{:S(2)}, u32[]{:S(2)}) collective-permute-start(bf16[160,2048]{1,0:T(8,128)(2,1)S(1)} %fusion.10), channel_id=1, source_target_pairs={{0,4},{8,0},{16,8},{24,16},{28,24},{20,28},{12,20},{4,12},{1,5},{9... | collective-permute-start | bytes 1966088 | tf_op jit(solution)/shard_map/ppermute | solution.py:92
  272.5 14.7 %collective-permute-start.45 = (bf16[160,2048]{1,0:T(8,128)(2,1)S(1)}, bf16[160,2048]{1,0:T(8,128)(2,1)S(1)}, u32[]{:S(2)}, u32[]{:S(2)}) collective-permute-start(bf16[160,2048]{1,0:T(8,128)(2,1)S(1)} %fusion.9), channel_id=1, source_target_pairs={{0,4},{8,0},{16,8},{24,16},{28,24},{20,28},{12,20},{4,12},{1,5},{9... | collective-permute-start | bytes 1966088 | tf_op jit(solution)/shard_map/ppermute | solution.py:92
  287.3 14.7 %collective-permute-start.46 = (bf16[160,2048]{1,0:T(8,128)(2,1)S(1)}, bf16[160,2048]{1,0:T(8,128)(2,1)S(1)}, u32[]{:S(2)}, u32[]{:S(2)}) collective-permute-start(bf16[160,2048]{1,0:T(8,128)(2,1)S(1)} %fusion.8), channel_id=1, source_target_pairs={{0,4},{8,0},{16,8},{24,16},{28,24},{20,28},{12,20},{4,12},{1,5},{9... | collective-permute-start | bytes 1966088 | tf_op jit(solution)/shard_map/ppermute | solution.py:92
  302.2 14.7 %collective-permute-start.47 = (bf16[160,2048]{1,0:T(8,128)(2,1)S(1)}, bf16[160,2048]{1,0:T(8,128)(2,1)S(1)}, u32[]{:S(2)}, u32[]{:S(2)}) collective-permute-start(bf16[160,2048]{1,0:T(8,128)(2,1)S(1)} %fusion.7), channel_id=1, source_target_pairs={{0,4},{8,0},{16,8},{24,16},{28,24},{20,28},{12,20},{4,12},{1,5},{9... | collective-permute-start | bytes 1966088 | tf_op jit(solution)/shard_map/ppermute | solution.py:92
  315.1 14.9 %collective-permute-start.41 = (bf16[160,2048]{1,0:T(8,128)(2,1)S(1)}, bf16[160,2048]{1,0:T(8,128)(2,1)S(1)}, u32[]{:S(2)}, u32[]{:S(2)}) collective-permute-start(bf16[160,2048]{1,0:T(8,128)(2,1)S(1)} %fusion.12), channel_id=1, source_target_pairs={{0,8},{8,16},{16,24},{24,28},{28,20},{20,12},{12,4},{4,0},{1,9},{9... | collective-permute-start | bytes 1966088 | tf_op jit(solution)/shard_map/ppermute | solution.py:91
  317.1 15.2 %collective-permute-start.48 = (bf16[160,2048]{1,0:T(8,128)(2,1)S(1)}, bf16[160,2048]{1,0:T(8,128)(2,1)S(1)}, u32[]{:S(2)}, u32[]{:S(2)}) collective-permute-start(bf16[160,2048]{1,0:T(8,128)(2,1)S(1)} %fusion.6), channel_id=1, source_target_pairs={{0,4},{8,0},{16,8},{24,16},{28,24},{20,28},{12,20},{4,12},{1,5},{9... | collective-permute-start | bytes 1966088 | tf_op jit(solution)/shard_map/ppermute | solution.py:92
  (45 other events, 454.1 us)
where the time goes:
time: 348 us; the launch traced here: 346 us
  waiting for transfers between devices  122 us (35%)
  starting transfers between devices  57.5 us (17%)
  other arithmetic  50 us (14%)
  between operations  37.1 us (11%)
  matrix products  35.2 us (10%)
  local copies, waits for them, and re-layouts  30.3 us (9%)
  blocking collectives  13.8 us (4%)
    ppermute x7, waiting for transfers between devices, ring_scatter(): got_left = lax.ppermute(send_left.astype(jnp.bfloat16), axis, forward)  55.9 us
    ppermute x7, waiting for transfers between devices, advance(): lax.ppermute(send_right.astype(jnp.bfloat16), self.axis, self.backward)  35.6 us
    ppermute x7, waiting for transfers between devices, direct_gather(): got[count - shift] = lax.ppermute(value, axis, pairs)  16.1 us
    dot_general x4, matrix products, against(): lax.dot_general(left, right, (((1,), (1,)), ((), ())), preferred_element_...  14.9 us
    ppermute x7, starting transfers between devices, direct_gather(): got[count - shift] = lax.ppermute(value, axis, pairs)  12.2 us
    ppermute x7, starting transfers between devices, direct_scatter(): lax.ppermute(blocks[shift].astype(jnp.bfloat16), axis, pairs)  11.9 us
    ppermute x7, starting transfers between devices, ring_scatter(): got_right = lax.ppermute(send_right.astype(jnp.bfloat16), axis, backward)  9.87 us
    convert_element_type x6, other arithmetic, ring_scatter(): got_left = lax.ppermute(send_left.astype(jnp.bfloat16), axis, forward)  8.84 us
  transfers between devices with their start and end apart: 50, of which 28 were waited for; matrix products, arithmetic and copies ran while one was open for 24% of the time, Pallas kernels for 0%

commit v1 on v0

--- a/solution.py
+++ b/solution.py
@@ -10,6 +10,24 @@
 THETA = 500000.0
 NEG = -1e30
 PIECE = 64
+
+
+def gather_around(array, axis, dim):
+    ways, here, turn = (lax.axis_size(axis), lax.axis_index(axis), array.shape[dim])
+    shape = [n * ways if d == dim else n for d, n in enumerate(array.shape)]
+    full = lax.dynamic_update_slice_in_dim(
+        jnp.zeros(shape, array.dtype), array, here * turn, axis=dim
+    )
+    going_up = going_down = array
+    for far in range(1, ways // 2 + 1):
+        going_up = lax.ppermute(going_up, axis, [(d, (d + 1) % ways) for d in range(ways)])
+        full = lax.dynamic_update_slice_in_dim(full, going_up, (here - far) % ways * turn, axis=dim)
+        if 2 * far < ways:
+            going_down = lax.ppermute(going_down, axis, [(d, (d - 1) % ways) for d in range(ways)])
+            full = lax.dynamic_update_slice_in_dim(
+                full, going_down, (here + far) % ways * turn, axis=dim
+            )
+    return full
 
 
 def angles(place, width):
@@ -339,7 +357,7 @@
     query_raw = rotate(query_grad, cosine_mine[:, None, :], -sine_mine[:, None, :]).reshape(
         rows_mine, heads_width
     )
-    query_rows = lax.all_gather(query_raw.astype(jnp.bfloat16), "tp", axis=0, tiled=True)
+    query_rows = gather_around(query_raw.astype(jnp.bfloat16), "tp", 0)
     d_qkv = jnp.concatenate(
         [query_rows, key_raw.astype(jnp.bfloat16), pair_grad[:, head_dim:].astype(jnp.bfloat16)],
         axis=1,

time: 348 us -> 360 us (1.034)
  waiting for transfers between devices: 122 us -> 139 us
  blocking collectives: 13.8 us -> 6.7 us
  starting transfers between devices: 57.5 us -> 61.5 us
    ppermute x7, waiting for transfers between devices: 4.4 us -> 49.8 us  [advance(): lax.ppermute(send_left.astype(jnp.bfloat16), self.axis, self.forward)]
    ppermute x7, waiting for transfers between devices: 35.6 us -> 7.26 us  [advance(): lax.ppermute(send_right.astype(jnp.bfloat16), self.axis, self.backward)]
    all_gather x1 -> x0, blocking collectives: 7.11 us -> none  [shards(): lax.all_gather(query_raw.astype(jnp.bfloat16), 'tp', axis=0, tiled=True)]
    ppermute x7, starting transfers between devices: 9.87 us -> 14.2 us  [ring_scatter(): got_right = lax.ppermute(send_right.astype(jnp.bfloat16), axis, backward)]
  transfers between devices with their start and end apart: 50 -> 53, of which waited for: 28 -> 27; matrix products, arithmetic and copies ran while one was open for 24% -> 23% of each run, Pallas kernels for 0% -> 0%
where the time goes in v1:
time: 360 us; the launch traced here: 358 us
  waiting for transfers between devices  139 us (39%)
  starting transfers between devices  61.5 us (17%)
  other arithmetic  49 us (14%)
  between operations  37 us (10%)
  matrix products  35 us (10%)
  local copies, waits for them, and re-layouts  30.2 us (8%)
  blocking collectives  6.7 us (2%)
    ppermute x7, waiting for transfers between devices, ring_scatter(): got_left = lax.ppermute(send_left.astype(jnp.bfloat16), axis, forward)  53.6 us
    ppermute x7, waiting for transfers between devices, advance(): lax.ppermute(send_left.astype(jnp.bfloat16), self.axis, self.forward)  49.8 us
    ppermute x7, waiting for transfers between devices, direct_gather(): got[count - shift] = lax.ppermute(value, axis, pairs)  16.1 us
    dot_general x4, matrix products, against(): lax.dot_general(left, right, (((1,), (1,)), ((), ())), preferred_element_...  14.9 us
    ppermute x7, starting transfers between devices, ring_scatter(): got_right = lax.ppermute(send_right.astype(jnp.bfloat16), axis, backward)  14.2 us
    ppermute x7, starting transfers between devices, direct_gather(): got[count - shift] = lax.ppermute(value, axis, pairs)  12.2 us
    ppermute x7, starting transfers between devices, direct_scatter(): lax.ppermute(blocks[shift].astype(jnp.bfloat16), axis, pairs)  11.9 us
    ppermute x7, starting transfers between devices, advance(): lax.ppermute(send_right.astype(jnp.bfloat16), self.axis, self.backward)  9.95 us
  transfers between devices with their start and end apart: 53, of which 27 were waited for; matrix products, arithmetic and copies ran while one was open for 23% of the time, Pallas kernels for 0%

profile of v1, /device:TPU:0, one launch (start us, length us, event | category | flops | bytes accessed | tf_op | source)
XLA Modules:
  0.0 358.3 jit_solution(13837964466086303119)
XLA Ops:
  2.2 6.9 %fusion.70 = f32[256,1280]{1,0:T(8,128)S(1)} fusion(bf16[256,4096]{1,0:T(8,128)(2,1)S(1)} %copy-done, bf16[1280,4096]{1,0:T(8,128)(2,1)} %param.13), kind=kOutput, calls=%fused_computation.176 | convolution fusion | flops 2684354560 | bytes 13893632 | tf_op jit(solution)/shard_map/dot_general | solution.py:50
  9.6 6.4 %convolution_convert_fusion.2 = bf16[256,1024]{1,0:T(8,128)(2,1)S(1)} fusion(bf16[256,4096]{1,0:T(8,128)(2,1)} %param.15, bf16[1024,4096]{1,0:T(8,128)(2,1)} %param.14), kind=kOutput, calls=%fused_computation.45 | convolution fusion | flops 2147745792 | bytes 11010048 | tf_op jit(solution)/shard_map/dot_general | solution.py:50
  37.9 4.2 %collective-permute-done.1 = f32[128,256]{1,0:T(8,128)S(1)} collective-permute-done((f32[128,256]{1,0:T(8,128)S(1)}, f32[128,256]{1,0:T(8,128)S(1)}, u32[]{:S(2)}, u32[]{:S(2)}) %collective-permute-start.1) | collective-permute-done | bytes 131104 | tf_op jit(solution)/shard_map/ppermute | solution.py:213
  44.3 4.6 %collective-permute-start.3 = (bf16[259,256]{1,0:T(8,128)(2,1)S(1)}, bf16[259,256]{1,0:T(8,128)(2,1)S(1)}, u32[]{:S(2)}, u32[]{:S(2)}) collective-permute-start(bf16[259,256]{1,0:T(8,128)(2,1)S(1)} %get-tuple-element.19), channel_id=1, source_target_pairs={{0,28},{4,0},{8,4},{12,8},{16,12},{20,16},{24,20},{28,24},{1,29},{... | collective-permute-start | bytes 397832 | tf_op jit(solution)/shard_map/ppermute | solution.py:242
  49.4 3.0 collective-permute-start.6
  58.8 13.5 %collective-permute-done.6 = bf16[259,256]{1,0:T(8,128)(2,1)S(1)} collective-permute-done((bf16[259,256]{1,0:T(8,128)(2,1)S(1)}, bf16[259,256]{1,0:T(8,128)(2,1)S(1)}, u32[]{:S(2)}, u32[]{:S(2)}) %collective-permute-start.6) | collective-permute-done | bytes 132640 | tf_op jit(solution)/shard_map/ppermute | solution.py:242
  89.0 6.7 %all_gather.3 = bf16[256,1024]{1,0:T(8,128)(2,1)S(1)} all-gather(bf16[64,1024]{1,0:T(8,128)(2,1)S(1)} %bitcast.247), channel_id=1, replica_groups=mesh['ctx'=8,'tp'=4] {'tp'}, dimensions={0}, use_global_device_ids=true | all-gather | bytes 655360 | tf_op jit(solution)/shard_map/all_gather | solution.py:338
  98.2 6.3 %fusion.65 = (f32[8,128,2048]{2,1,0:T(8,128)}, f32[8,128,2048]{2,1,0:T(8,128)}) fusion(f32[8,128,4096]{2,1,0:T(8,128)S(1)} %bitcast.236), kind=kLoop, calls=%fused_computation.171 | loop fusion | bytes 33554432 | tf_op jit(solution)/shard_map/slice | solution.py:173
  106.8 2.9 collective-permute-start.26
  134.5 7.2 %collective-permute-done.19 = bf16[128,2048]{1,0:T(8,128)(2,1)S(1)} collective-permute-done((bf16[128,2048]{1,0:T(8,128)(2,1)S(1)}, bf16[128,2048]{1,0:T(8,128)(2,1)S(1)}, u32[]{:S(2)}, u32[]{:S(2)}) %collective-permute-start.19) | collective-permute-done | bytes 524320 | tf_op jit(solution)/shard_map/ppermute | solution.py:188
  171.7 11.3 %collective-permute-done.29 = bf16[128,2048]{1,0:T(8,128)(2,1)S(1)} collective-permute-done((bf16[128,2048]{1,0:T(8,128)(2,1)}, bf16[128,2048]{1,0:T(8,128)(2,1)S(1)}, u32[]{:S(2)}, u32[]{:S(2)}) %collective-permute-start.29) | collective-permute-done | bytes 524320 | tf_op jit(solution)/shard_map/ppermute | solution.py:187
  187.9 10.6 %collective-permute-done.30 = bf16[128,2048]{1,0:T(8,128)(2,1)S(1)} collective-permute-done((bf16[128,2048]{1,0:T(8,128)(2,1)S(1)}, bf16[128,2048]{1,0:T(8,128)(2,1)S(1)}, u32[]{:S(2)}, u32[]{:S(2)}) %collective-permute-start.30) | collective-permute-done | bytes 524320 | tf_op jit(solution)/shard_map/ppermute | solution.py:187
  204.2 8.8 %collective-permute-done.31 = bf16[128,2048]{1,0:T(8,128)(2,1)S(1)} collective-permute-done((bf16[128,2048]{1,0:T(8,128)(2,1)S(1)}, bf16[128,2048]{1,0:T(8,128)(2,1)S(1)}, u32[]{:S(2)}, u32[]{:S(2)}) %collective-permute-start.31) | collective-permute-done | bytes 524320 | tf_op jit(solution)/shard_map/ppermute | solution.py:187
  220.5 7.4 %collective-permute-done.32 = bf16[128,2048]{1,0:T(8,128)(2,1)} collective-permute-done((bf16[128,2048]{1,0:T(8,128)(2,1)}, bf16[128,2048]{1,0:T(8,128)(2,1)}, u32[]{:S(2)}, u32[]{:S(2)}) %collective-permute-start.32) | collective-permute-done | bytes 524320 | tf_op jit(solution)/shard_map/ppermute | solution.py:187
  234.0 6.9 %collective-permute-done.33 = bf16[128,2048]{1,0:T(8,128)(2,1)S(1)} collective-permute-done((bf16[128,2048]{1,0:T(8,128)(2,1)S(1)}, bf16[128,2048]{1,0:T(8,128)(2,1)S(1)}, u32[]{:S(2)}, u32[]{:S(2)}) %collective-permute-start.33) | collective-permute-done | bytes 524320 | tf_op jit(solution)/shard_map/ppermute | solution.py:187
  242.2 8.1 %fusion.64 = (f32[8,160,2048]{2,1,0:T(8,128)}, f32[8,160,2048]{2,1,0:T(8,128)}) fusion(f32[8,160,4096]{2,1,0:T(8,128)S(1)} %bitcast.235), kind=kLoop, calls=%fused_computation.170 | loop fusion | bytes 41943040 | tf_op jit(solution)/shard_map/slice | solution.py:98
  255.9 9.4 %collective-permute-done.39 = bf16[160,2048]{1,0:T(8,128)(2,1)S(1)} collective-permute-done((bf16[160,2048]{1,0:T(8,128)(2,1)S(1)}, bf16[160,2048]{1,0:T(8,128)(2,1)S(1)}, u32[]{:S(2)}, u32[]{:S(2)}) %collective-permute-start.39) | collective-permute-done | bytes 655392 | tf_op jit(solution)/shard_map/ppermute | solution.py:109
  270.6 9.5 %collective-permute-done.40 = bf16[160,2048]{1,0:T(8,128)(2,1)S(1)} collective-permute-done((bf16[160,2048]{1,0:T(8,128)(2,1)S(1)}, bf16[160,2048]{1,0:T(8,128)(2,1)S(1)}, u32[]{:S(2)}, u32[]{:S(2)}) %collective-permute-start.40) | collective-permute-done | bytes 655392 | tf_op jit(solution)/shard_map/ppermute | solution.py:109
  285.5 9.5 %collective-permute-done.41 = bf16[160,2048]{1,0:T(8,128)(2,1)S(1)} collective-permute-done((bf16[160,2048]{1,0:T(8,128)(2,1)S(1)}, bf16[160,2048]{1,0:T(8,128)(2,1)S(1)}, u32[]{:S(2)}, u32[]{:S(2)}) %collective-permute-start.41) | collective-permute-done | bytes 655392 | tf_op jit(solution)/shard_map/ppermute | solution.py:109
  300.4 9.5 %collective-permute-done.42 = bf16[160,2048]{1,0:T(8,128)(2,1)S(1)} collective-permute-done((bf16[160,2048]{1,0:T(8,128)(2,1)S(1)}, bf16[160,2048]{1,0:T(8,128)(2,1)S(1)}, u32[]{:S(2)}, u32[]{:S(2)}) %collective-permute-start.42) | collective-permute-done | bytes 655392 | tf_op jit(solution)/shard_map/ppermute | solution.py:109
  315.3 7.6 %convolution_convert_fusion = bf16[256,4096]{1,0:T(8,128)(2,1)} fusion(bf16[256,1024]{1,0:T(8,128)(2,1)S(1)} %all_gather.3, bf16[1024,4096]{1,0:T(8,128)(2,1)} %param.14), kind=kOutput, calls=%fused_computation.3 | convolution fusion | flops 2148532224 | bytes 11010048 | tf_op jit(solution)/shard_map/dot_general | solution.py:339
  331.1 4.1 %convolution_convert_fusion.1 = bf16[256,4096]{1,0:T(8,128)(2,1)} fusion(bf16[256,1280]{1,0:T(8,128)(2,1)S(1)} %concatenate.45, bf16[1280,4096]{1,0:T(8,128)(2,1)S(1)} %bitcast.254), kind=kOutput, calls=%fused_computation.4 | convolution fusion | flops 2685403136 | bytes 13238272 | tf_op jit(solution)/shard_map/dot_general | solution.py:365
  335.2 7.3 %collective-permute-done.44 = bf16[160,2048]{1,0:T(8,128)(2,1)S(1)} collective-permute-done((bf16[160,2048]{1,0:T(8,128)(2,1)S(1)}, bf16[160,2048]{1,0:T(8,128)(2,1)S(1)}, u32[]{:S(2)}, u32[]{:S(2)}) %collective-permute-start.44) | collective-permute-done | bytes 655392 | tf_op jit(solution)/shard_map/ppermute | solution.py:109
  349.1 5.6 %collective-permute-done.45 = bf16[160,2048]{1,0:T(8,128)(2,1)S(1)} collective-permute-done((bf16[160,2048]{1,0:T(8,128)(2,1)S(1)}, bf16[160,2048]{1,0:T(8,128)(2,1)S(1)}, u32[]{:S(2)}, u32[]{:S(2)}) %collective-permute-start.45) | collective-permute-done | bytes 655392 | tf_op jit(solution)/shard_map/ppermute | solution.py:109
  (231 shorter events, 143.9 us)
Async XLA Ops:
  9.1 25.8 %collective-permute-start = (f32[256,1280]{1,0:T(8,128)S(1)}, f32[256,1280]{1,0:T(8,128)}, u32[]{:S(2)}, u32[]{:S(2)}) collective-permute-start(f32[256,1280]{1,0:T(8,128)S(1)} %fusion.70), channel_id=1, source_target_pairs={{0,1},{1,0},{2,3},{3,2},{4,5},{5,4},{6,7},{7,6},{8,9},{9,8},{10,11... | collective-permute-start | bytes 3932168 | tf_op jit(solution)/shard_map/ppermute | solution.py:205
  17.6 19.0 %collective-permute-start.11 = (bf16[128,1024]{1,0:T(8,128)(2,1)}, bf16[128,1024]{1,0:T(8,128)(2,1)}, u32[]{:S(2)}, u32[]{:S(2)}) collective-permute-start(bf16[128,1024]{1,0:T(8,128)(2,1)} %constant_dynamic-slice_fusion), channel_id=1, source_target_pairs={{0,2},{1,3},{2,0},{3,1},{4,6},{5,7},{6,4},{7,5},{8,10},{9,11},{10,... | collective-permute-start | bytes 786440 | tf_op jit(solution)/shard_map/ppermute | solution.py:228
  49.4 22.9 %collective-permute-start.6 = (bf16[259,256]{1,0:T(8,128)(2,1)S(1)}, bf16[259,256]{1,0:T(8,128)(2,1)S(1)}, u32[]{:S(2)}, u32[]{:S(2)}) collective-permute-start(bf16[259,256]{1,0:T(8,128)(2,1)S(1)} %get-tuple-element.19), channel_id=1, source_target_pairs={{0,16},{4,20},{8,24},{12,28},{16,0},{20,4},{24,8},{28,12},{1,17},{... | collective-permute-start | bytes 397832 | tf_op jit(solution)/shard_map/ppermute | solution.py:242
  53.0 20.7 %collective-permute-start.7 = (bf16[259,256]{1,0:T(8,128)(2,1)S(1)}, bf16[259,256]{1,0:T(8,128)(2,1)S(1)}, u32[]{:S(2)}, u32[]{:S(2)}) collective-permute-start(bf16[259,256]{1,0:T(8,128)(2,1)S(1)} %get-tuple-element.19), channel_id=1, source_target_pairs={{0,12},{4,16},{8,20},{12,24},{16,28},{20,0},{24,4},{28,8},{1,13},{... | collective-permute-start | bytes 397832 | tf_op jit(solution)/shard_map/ppermute | solution.py:242
  54.2 19.6 %collective-permute-start.8 = (bf16[259,256]{1,0:T(8,128)(2,1)S(1)}, bf16[259,256]{1,0:T(8,128)(2,1)S(1)}, u32[]{:S(2)}, u32[]{:S(2)}) collective-permute-start(bf16[259,256]{1,0:T(8,128)(2,1)S(1)} %get-tuple-element.19), channel_id=1, source_target_pairs={{0,8},{4,12},{8,16},{12,20},{16,24},{20,28},{24,0},{28,4},{1,9},{5... | collective-permute-start | bytes 397832 | tf_op jit(solution)/shard_map/ppermute | solution.py:242
  55.9 17.9 %collective-permute-start.9 = (bf16[259,256]{1,0:T(8,128)(2,1)S(1)}, bf16[259,256]{1,0:T(8,128)(2,1)S(1)}, u32[]{:S(2)}, u32[]{:S(2)}) collective-permute-start(bf16[259,256]{1,0:T(8,128)(2,1)S(1)} %get-tuple-element.19), channel_id=1, source_target_pairs={{0,4},{4,8},{8,12},{12,16},{16,20},{20,24},{24,28},{28,0},{1,5},{5... | collective-permute-start | bytes 397832 | tf_op jit(solution)/shard_map/ppermute | solution.py:242
  82.3 22.2 %collective-permute-start.20 = (bf16[256,256]{1,0:T(8,128)(2,1)}, bf16[256,256]{1,0:T(8,128)(2,1)}, u32[]{:S(2)}, u32[]{:S(2)}) collective-permute-start(bf16[256,256]{1,0:T(8,128)(2,1)} %get-tuple-element.30), channel_id=1, source_target_pairs={{0,4},{4,8},{8,12},{12,16},{16,20},{20,24},{24,28},{28,0},{1,5},{5... | collective-permute-start | bytes 393224 | tf_op jit(solution)/shard_map/ppermute | solution.py:253
  82.3 24.6 %collective-permute-start.21 = (bf16[256,256]{1,0:T(8,128)(2,1)}, bf16[256,256]{1,0:T(8,128)(2,1)}, u32[]{:S(2)}, u32[]{:S(2)}) collective-permute-start(bf16[256,256]{1,0:T(8,128)(2,1)} %get-tuple-element.36), channel_id=1, source_target_pairs={{0,8},{4,12},{8,16},{12,20},{16,24},{20,28},{24,0},{28,4},{1,9},{5... | collective-permute-start | bytes 393224 | tf_op jit(solution)/shard_map/ppermute | solution.py:253
  83.2 28.7 %collective-permute-start.22 = (bf16[256,256]{1,0:T(8,128)(2,1)}, bf16[256,256]{1,0:T(8,128)(2,1)}, u32[]{:S(2)}, u32[]{:S(2)}) collective-permute-start(bf16[256,256]{1,0:T(8,128)(2,1)} %get-tuple-element.35), channel_id=1, source_target_pairs={{0,12},{4,16},{8,20},{12,24},{16,28},{20,0},{24,4},{28,8},{1,13},{... | collective-permute-start | bytes 393224 | tf_op jit(solution)/shard_map/ppermute | solution.py:253
  86.0 25.9 %collective-permute-start.23 = (bf16[256,256]{1,0:T(8,128)(2,1)}, bf16[256,256]{1,0:T(8,128)(2,1)}, u32[]{:S(2)}, u32[]{:S(2)}) collective-permute-start(bf16[256,256]{1,0:T(8,128)(2,1)} %get-tuple-element.34), channel_id=1, source_target_pairs={{0,16},{4,20},{8,24},{12,28},{16,0},{20,4},{24,8},{28,12},{1,17},{... | collective-permute-start | bytes 393224 | tf_op jit(solution)/shard_map/ppermute | solution.py:253
  87.6 24.3 %collective-permute-start.24 = (bf16[256,256]{1,0:T(8,128)(2,1)}, bf16[256,256]{1,0:T(8,128)(2,1)}, u32[]{:S(2)}, u32[]{:S(2)}) collective-permute-start(bf16[256,256]{1,0:T(8,128)(2,1)} %get-tuple-element.33), channel_id=1, source_target_pairs={{0,20},{4,24},{8,28},{12,0},{16,4},{20,8},{24,12},{28,16},{1,21},{... | collective-permute-start | bytes 393224 | tf_op jit(solution)/shard_map/ppermute | solution.py:253
  111.9 14.6 %collective-permute-start.18 = (bf16[128,2048]{1,0:T(8,128)(2,1)}, bf16[128,2048]{1,0:T(8,128)(2,1)}, u32[]{:S(2)}, u32[]{:S(2)}) collective-permute-start(bf16[128,2048]{1,0:T(8,128)(2,1)} %fusion.31), channel_id=1, source_target_pairs={{0,4},{8,0},{16,8},{24,16},{28,24},{20,28},{12,20},{4,12},{1,5},{9... | collective-permute-start | bytes 1572872 | tf_op jit(solution)/shard_map/ppermute | solution.py:188
  148.9 19.6 %collective-permute-start.34 = (bf16[128,2048]{1,0:T(8,128)(2,1)}, bf16[128,2048]{1,0:T(8,128)(2,1)}, u32[]{:S(2)}, u32[]{:S(2)}) collective-permute-start(bf16[128,2048]{1,0:T(8,128)(2,1)} %bitcast_add_fusion.24), channel_id=1, source_target_pairs={{0,4},{8,0},{16,8},{24,16},{28,24},{20,28},{12,20},{4,12},{1,5},{9... | collective-permute-start | bytes 1572872 | tf_op jit(solution)/shard_map/ppermute | solution.py:188
  150.9 17.1 %collective-permute-start.13 = (bf16[64,1024]{1,0:T(8,128)(2,1)S(1)}, bf16[64,1024]{1,0:T(8,128)(2,1)S(1)}, u32[]{:S(2)}, u32[]{:S(2)}) collective-permute-start(bf16[64,1024]{1,0:T(8,128)(2,1)S(1)} %copy_bitcast_fusion.1), channel_id=1, source_target_pairs={{0,1},{1,2},{2,3},{3,0},{4,5},{5,6},{6,7},{7,4},{8,9},{9,10},{10,1... | collective-permute-start | bytes 393224 | tf_op jit(solution)/shard_map/ppermute | solution.py:23
  166.1 18.6 %collective-permute-start.14 = (bf16[64,1024]{1,0:T(8,128)(2,1)S(1)}, bf16[64,1024]{1,0:T(8,128)(2,1)S(1)}, u32[]{:S(2)}, u32[]{:S(2)}) collective-permute-start(bf16[64,1024]{1,0:T(8,128)(2,1)S(1)} %copy_bitcast_fusion.1), channel_id=1, source_target_pairs={{0,3},{1,0},{2,1},{3,2},{4,7},{5,4},{6,5},{7,6},{8,11},{9,8},{10,9... | collective-permute-start | bytes 393224 | tf_op jit(solution)/shard_map/ppermute | solution.py:26
  168.0 32.1 %collective-permute-start.15 = (bf16[64,1024]{1,0:T(8,128)(2,1)S(1)}, bf16[64,1024]{1,0:T(8,128)(2,1)S(1)}, u32[]{:S(2)}, u32[]{:S(2)}) collective-permute-start(bf16[64,1024]{1,0:T(8,128)(2,1)S(1)} %collective-permute-done.13), channel_id=1, source_target_pairs={{0,1},{1,2},{2,3},{3,0},{4,5},{5,6},{6,7},{7,4},{8,9},{9,10},{10,1... | collective-permute-start | bytes 393224 | tf_op jit(solution)/shard_map/ppermute | solution.py:23
  168.1 15.0 %collective-permute-start.29 = (bf16[128,2048]{1,0:T(8,128)(2,1)}, bf16[128,2048]{1,0:T(8,128)(2,1)S(1)}, u32[]{:S(2)}, u32[]{:S(2)}) collective-permute-start(bf16[128,2048]{1,0:T(8,128)(2,1)} %bitcast_add_fusion.26), channel_id=1, source_target_pairs={{0,8},{8,16},{16,24},{24,28},{28,20},{20,12},{12,4},{4,0},{1,9},{9... | collective-permute-start | bytes 1572872 | tf_op jit(solution)/shard_map/ppermute | solution.py:187
  169.9 14.8 %collective-permute-start.35 = (bf16[128,2048]{1,0:T(8,128)(2,1)S(1)}, bf16[128,2048]{1,0:T(8,128)(2,1)S(1)}, u32[]{:S(2)}, u32[]{:S(2)}) collective-permute-start(bf16[128,2048]{1,0:T(8,128)(2,1)S(1)} %fusion.21), channel_id=1, source_target_pairs={{0,4},{8,0},{16,8},{24,16},{28,24},{20,28},{12,20},{4,12},{1,5},{9... | collective-permute-start | bytes 1572872 | tf_op jit(solution)/shard_map/ppermute | solution.py:188
  202.5 14.8 %collective-permute-start.37 = (bf16[128,2048]{1,0:T(8,128)(2,1)}, bf16[128,2048]{1,0:T(8,128)(2,1)}, u32[]{:S(2)}, u32[]{:S(2)}) collective-permute-start(bf16[128,2048]{1,0:T(8,128)(2,1)} %fusion.19), channel_id=1, source_target_pairs={{0,4},{8,0},{16,8},{24,16},{28,24},{20,28},{12,20},{4,12},{1,5},{9... | collective-permute-start | bytes 1572872 | tf_op jit(solution)/shard_map/ppermute | solution.py:188
  268.7 14.7 %collective-permute-start.47 = (bf16[160,2048]{1,0:T(8,128)(2,1)S(1)}, bf16[160,2048]{1,0:T(8,128)(2,1)S(1)}, u32[]{:S(2)}, u32[]{:S(2)}) collective-permute-start(bf16[160,2048]{1,0:T(8,128)(2,1)S(1)} %fusion.10), channel_id=1, source_target_pairs={{0,4},{8,0},{16,8},{24,16},{28,24},{20,28},{12,20},{4,12},{1,5},{9... | collective-permute-start | bytes 1966088 | tf_op jit(solution)/shard_map/ppermute | solution.py:110
  283.6 14.7 %collective-permute-start.48 = (bf16[160,2048]{1,0:T(8,128)(2,1)S(1)}, bf16[160,2048]{1,0:T(8,128)(2,1)S(1)}, u32[]{:S(2)}, u32[]{:S(2)}) collective-permute-start(bf16[160,2048]{1,0:T(8,128)(2,1)S(1)} %fusion.9), channel_id=1, source_target_pairs={{0,4},{8,0},{16,8},{24,16},{28,24},{20,28},{12,20},{4,12},{1,5},{9... | collective-permute-start | bytes 1966088 | tf_op jit(solution)/shard_map/ppermute | solution.py:110
  313.1 15.7 %collective-permute-start.50 = (bf16[160,2048]{1,0:T(8,128)(2,1)S(1)}, bf16[160,2048]{1,0:T(8,128)(2,1)S(1)}, u32[]{:S(2)}, u32[]{:S(2)}) collective-permute-start(bf16[160,2048]{1,0:T(8,128)(2,1)S(1)} %fusion.7), channel_id=1, source_target_pairs={{0,4},{8,0},{16,8},{24,16},{28,24},{20,28},{12,20},{4,12},{1,5},{9... | collective-permute-start | bytes 1966088 | tf_op jit(solution)/shard_map/ppermute | solution.py:110
  327.2 15.3 %collective-permute-start.44 = (bf16[160,2048]{1,0:T(8,128)(2,1)S(1)}, bf16[160,2048]{1,0:T(8,128)(2,1)S(1)}, u32[]{:S(2)}, u32[]{:S(2)}) collective-permute-start(bf16[160,2048]{1,0:T(8,128)(2,1)S(1)} %fusion.12), channel_id=1, source_target_pairs={{0,8},{8,16},{16,24},{24,28},{28,20},{20,12},{12,4},{4,0},{1,9},{9... | collective-permute-start | bytes 1966088 | tf_op jit(solution)/shard_map/ppermute | solution.py:109
  329.0 16.3 %collective-permute-start.51 = (bf16[160,2048]{1,0:T(8,128)(2,1)S(1)}, bf16[160,2048]{1,0:T(8,128)(2,1)S(1)}, u32[]{:S(2)}, u32[]{:S(2)}) collective-permute-start(bf16[160,2048]{1,0:T(8,128)(2,1)S(1)} %fusion.6), channel_id=1, source_target_pairs={{0,4},{8,0},{16,8},{24,16},{28,24},{20,28},{12,20},{4,12},{1,5},{9... | collective-permute-start | bytes 1966088 | tf_op jit(solution)/shard_map/ppermute | solution.py:110
  (48 other events, 543.0 us)
